TPU v7x, 256 devices: a whole 4x4x8 slice. The times are simulated.
256 devices in a mesh: tm: 32 (over y, x, core), tensor: 8 (over z).
Axes of the slice: x: 4, y: 4, z: 8, core: 2. Of those that a mesh axis runs over, the one named last changes fastest.
Arguments:
- features: bfloat16 [32768, 1536], P(('tm', 'tensor')), may hold values from -4 to 4
- frame_mask: int32 [32768], P('tm'), may hold values 0 or 1
- total_length: int32 [1], replicated, may hold values from 24576 to 32768
- norm_gain: float32 [1536], replicated, may hold values from 0.1 to 1.9
- value_weight: bfloat16 [1536, 1536], P(None, 'tensor'), may hold values from -0.15625 to 0.15625
- gate_weight: bfloat16 [1536, 1536], P(None, 'tensor'), may hold values from -0.15625 to 0.15625
- depth_kernel: float32 [31, 1536], P(None, 'tensor'), may hold values from -1 to 1
- batch_gain: float32 [1536], P('tensor'), may hold values from 0.1 to 1.9
- batch_bias: float32 [1536], P('tensor'), may hold values from -2 to 2
- out_weight: bfloat16 [1536, 1536], P('tensor'), may hold values from -0.15625 to 0.15625
- feed_gain: float32 [1536], replicated, may hold values from 0.1 to 1.9
- up_weight: bfloat16 [1536, 6144], P('tm', 'tensor'), may hold values from -0.15625 to 0.15625
- down_weight: bfloat16 [6144, 1536], P('tensor', 'tm'), may hold values from -0.078125 to 0.078125
Outputs:
- encoded: bfloat16 [32768, 1536], P(('tm', 'tensor'))
All inputs are finite; a program needn't handle non-finite values. No bound on the sum of `frame_mask` on one device may be relied on, other than what follows from the above.
Results may differ from a plain program's by a relative error of at most 0.0074.
Values may be sent and summed in bfloat16 or wider, within the bound.
No kernel may reach another device: no remote copies, remote signals or barrier semaphores. Data moves between devices by JAX's collectives and lax.ppermute only.
A program may use at most 64 MiB of HBM per device.

v0:
```python
import jax
import jax.numpy as jnp
from jax import lax
from jax.sharding import PartitionSpec as P

KERNEL = 31


def extended(array, sides, width):
    for axis, dim in sides:
        devices, length = (lax.axis_size(axis), array.shape[dim])
        up = [(i, (i + 1) % devices) for i in range(devices - 1)]
        down = [(j, i) for i, j in up]
        last = lax.slice_in_dim(array, length - width, length, axis=dim)
        initial = lax.slice_in_dim(array, 0, width, axis=dim)
        before = lax.ppermute(last, axis, up)
        after = lax.ppermute(initial, axis, down)
        array = jnp.concatenate([before, array, after], axis=dim)
    return array


def layer_norm(rows, gain):
    values = rows.astype(jnp.float32)
    centre = jnp.mean(values, axis=-1, keepdims=True)
    spread = jnp.mean(jnp.square(values - centre), axis=-1, keepdims=True)
    return (values - centre) * lax.rsqrt(spread + 1e-05) * gain


def merge_moments(low, high):
    n_a, mean_a, m2_a = (low[0], low[1], low[2])
    n_b, mean_b, m2_b = (high[0], high[1], high[2])
    n = n_a + n_b
    share = jnp.where(n > 0, n_b / jnp.maximum(n, 1.0), 0.0)
    delta = mean_b - mean_a
    mean = mean_a + delta * share
    m2 = m2_a + m2_b + jnp.square(delta) * n_a * share
    return jnp.stack([n, mean, m2])


def moments_over(stats, axis):
    size = lax.axis_size(axis)
    me = lax.axis_index(axis)
    step = 1
    while step < size:
        pairs = [(i, i ^ step) for i in range(size)]
        other = lax.ppermute(stats, axis, pairs)
        mine_low = me & step == 0
        low = jnp.where(mine_low, stats, other)
        high = jnp.where(mine_low, other, stats)
        stats = merge_moments(low, high)
        step *= 2
    return stats


def shards(
    features,
    frame_mask,
    total_length,
    norm_gain,
    value_weight,
    gate_weight,
    depth_kernel,
    batch_gain,
    batch_bias,
    out_weight,
    feed_gain,
    up_weight,
    down_weight,
):
    own_rows = features.shape[0]
    block = own_rows * lax.axis_size("tensor")
    positions = lax.axis_index("tm") * block + jnp.arange(block, dtype=jnp.int32)
    valid = ((frame_mask > 0) & (positions < total_length[0])).astype(jnp.float32)
    normed = layer_norm(features, norm_gain).astype(jnp.bfloat16)
    piece = lax.all_gather(normed, "tensor", axis=0, tiled=True)
    up_whole = lax.all_gather(up_weight, "tm", axis=0, tiled=True)
    down_whole = lax.all_gather(down_weight, "tm", axis=1, tiled=True)
    value = jnp.dot(piece, value_weight, preferred_element_type=jnp.float32)
    gate = jnp.dot(piece, gate_weight, preferred_element_type=jnp.float32)
    glu = (value * jax.nn.sigmoid(gate) * valid[:, None]).astype(jnp.bfloat16)
    padded = extended(glu, (("tm", 0),), KERNEL // 2)
    conv = jnp.zeros(glu.shape, jnp.float32)
    for tap in range(KERNEL):
        conv = conv + padded[tap : tap + block].astype(jnp.float32) * depth_kernel[tap]
    count_local = jnp.sum(valid)
    local_sum = jnp.sum(conv * valid[:, None], axis=0)
    local_mean = jnp.where(count_local > 0, local_sum / jnp.maximum(count_local, 1.0), 0.0)
    local_m2 = jnp.sum(jnp.square(conv - local_mean) * valid[:, None], axis=0)
    stats = jnp.stack([jnp.broadcast_to(count_local, local_sum.shape), local_mean, local_m2])
    stats = moments_over(stats, "tm")
    count, mean, m2 = (stats[0], stats[1], stats[2])
    centred = conv - mean
    var = m2 / count
    scaled = centred * lax.rsqrt(var + 1e-05) * batch_gain + batch_bias
    swished = (scaled * jax.nn.sigmoid(scaled)).astype(jnp.bfloat16)
    conv_part = jnp.dot(swished, out_weight, preferred_element_type=jnp.float32)
    conv_part, up_whole, down_whole = lax.optimization_barrier((conv_part, up_whole, down_whole))
    conv_out = lax.psum_scatter(
        conv_part.astype(jnp.bfloat16), "tensor", scatter_dimension=0, tiled=True
    ).astype(jnp.float32)
    mid = (features.astype(jnp.float32) + conv_out).astype(jnp.bfloat16)
    feed_normed = layer_norm(mid, feed_gain).astype(jnp.bfloat16)
    feed_block = lax.all_gather(feed_normed, "tensor", axis=0, tiled=True)
    pre = jnp.dot(feed_block, up_whole, preferred_element_type=jnp.float32)
    hidden = (pre * jax.nn.sigmoid(pre)).astype(jnp.bfloat16)
    partial_out = jnp.dot(hidden, down_whole, preferred_element_type=jnp.float32)
    feed_out = lax.psum_scatter(
        partial_out.astype(jnp.bfloat16), "tensor", scatter_dimension=0, tiled=True
    ).astype(jnp.float32)
    return (mid.astype(jnp.float32) + 0.5 * feed_out).astype(jnp.bfloat16)


def solution(mesh):
    placed = (
        P(("tm", "tensor"), None),
        P("tm"),
        P(),
        P(),
        P(None, "tensor"),
        P(None, "tensor"),
        P(None, "tensor"),
        P("tensor"),
        P("tensor"),
        P("tensor", None),
        P(),
        P("tm", "tensor"),
        P("tensor", "tm"),
    )
    return jax.shard_map(
        shards, mesh=mesh, in_specs=placed, out_specs=P(("tm", "tensor"), None), check_vma=False
    )
```

profile of v0, /device:TPU:2, one launch (start us, length us, event | category | flops | bytes accessed | tf_op | source)
XLA Modules:
  0.0 321.7 jit_solution(17575117318898476684)
XLA Ops:
  6.5 0.0 copy-start
  6.5 0.0 all-gather.5.cloned.1.call-start
  6.5 1.2 convert_reduce_fusion.1
  7.7 1.2 fusion.13
  9.0 2.0 fusion.15
  11.0 0.0 all-gather.5.cloned.1.call-update
  11.1 0.0 all-gather.7.cloned.1.call-start
  11.1 0.7 all-gather.7.cloned.1.call-update
  11.8 0.0 all-gather.9.cloned.1.call-start
  11.8 0.7 all-gather.9.cloned.1.call-update
  12.5 0.0 reduce-scatter.3.cloned.1.call-start
  13.2 1.0 fusion.66
  14.3 1.4 fusion.63
  15.6 0.0 copy-start.4
  15.6 43.5 %all-gather.5.cloned.1.call-done = bf16[1024,1536]{1,0:T(8,128)(2,1)} async-done(((bf16[128,1536]{1,0:T(8,128)(2,1)}), bf16[1024,1536]{1,0:T(8,128)(2,1)}) %all-gather.5.cloned.1.call-update) | async-done | bytes 3145744 | tf_op jit(solution)/shard_map/all_gather | solution.py:75
  59.1 0.0 copy-start.3
  59.1 3.4 %fusion.4 = f32[1024,192]{0,1:T(8,128)S(1)} fusion(bf16[1024,1536]{1,0:T(8,128)(2,1)} %all-gather.5.cloned.1.call-done, bf16[1536,192]{0,1:T(8,128)(2,1)} %param.18), kind=kOutput, calls=%fused_computation.36 | convolution fusion | flops 604569600 | bytes 4521984 | tf_op jit(solution)/shard_map/dot_general | solution.py:79
  62.5 0.0 copy-done.4
  62.6 0.0 copy-done.3
  62.6 0.0 copy-start.5
  62.6 0.0 copy-start.6
  62.6 1.2 fusion.5
  63.8 0.1 fusion.65
  63.9 1.9 collective-permute-start
  65.8 3.6 %collective-permute-start.1 = (bf16[15,192]{0,1:T(8,128)(2,1)S(1)}, bf16[15,192]{0,1:T(8,128)(2,1)S(1)}, u32[]{:S(2)}, u32[]{:S(2)}) collective-permute-start(bf16[15,192]{0,1:T(8,128)(2,1)S(1)} %get-tuple-element.32), channel_id=1, source_target_pairs={{8,0},{16,8},{24,16},{32,24},{40,32},{48,40},{56,48},{64,56},{72,6... | collective-permute-start | bytes 17288 | tf_op jit(solution)/shard_map/ppermute | solution.py:17
  69.4 1.0 fusion.67
  71.7 0.6 pad.12.clone
  72.3 0.0 collective-permute-done
  72.3 0.0 collective-permute-done.1
  72.4 5.6 %multiply_reduce_fusion.1 = (f32[192]{0:T(256)S(1)}, f32[1024,192]{0,1:T(8,128)S(1)}) fusion(f32[1024]{0:T(1024)S(1)} %get-tuple-element.28, f32[192]{0:T(256)S(1)} %bitcast.79, bf16[15,192]{0,1:T(8,128)(2,1)S(1)} %collective-permute-done.1, bf16[1024,192]{0,1:T(8,128)(2,1)S(1)} %fusion.5, f32[192]{0:T(256)S(1)} %bitcast.80, f32[192]{0:T(256)S(1)} %bitcast.51, ...), kind=kLoop, calls=%fused_computation.58 | loop fusion | flops 36175680 | bytes 1219840 | tf_op jit(solution)/shard_map/reduce_sum | solution.py:86
  78.0 0.3 multiply_reduce_fusion
  78.2 0.1 pad_maximum_fusion.2
  78.3 0.4 collective-permute-start.2
  78.7 0.8 collective-permute-done.2
  79.6 0.1 broadcast_select_fusion.1
  79.7 0.6 collective-permute-start.3
  80.3 3.1 collective-permute-done.3
  83.5 4.3 %collective-permute-start.4 = (f32[3,192]{1,0:T(4,128)S(1)}, f32[3,192]{1,0:T(4,128)S(1)}, u32[]{:S(2)}, u32[]{:S(2)}) collective-permute-start(f32[3,192]{1,0:T(4,128)S(1)} %pad_maximum_fusion.4), channel_id=1, source_target_pairs={{0,32},{8,40},{16,48},{24,56},{32,0},{40,8},{48,16},{56,24},{64,96... | collective-permute-start | bytes 6920 | tf_op jit(solution)/shard_map/ppermute | solution.py:46
  87.7 1.6 collective-permute-done.4
  89.4 1.6 collective-permute-start.5
  91.0 2.1 collective-permute-done.5
  93.2 3.2 collective-permute-start.6
  96.4 2.3 collective-permute-done.6
  98.7 0.0 copy-done
  98.7 0.0 copy-done.5
  98.7 0.0 copy-done.6
  98.7 2.9 fusion.18
  101.6 7.7 %all-gather.7.cloned.1.call-done = bf16[1536,768]{1,0:T(8,128)(2,1)} async-done(((bf16[48,768]{1,0:T(8,128)(2,1)}), bf16[1536,768]{1,0:T(8,128)(2,1)}) %all-gather.7.cloned.1.call-update) | async-done | bytes 2359312 | tf_op jit(solution)/shard_map/all_gather | solution.py:76
  109.3 51.2 %all-gather.9.cloned.1.call-done = bf16[768,1536]{0,1:T(8,128)(2,1)} async-done(((bf16[768,48]{0,1:T(8,128)(2,1)}), bf16[768,1536]{0,1:T(8,128)(2,1)}) %all-gather.9.cloned.1.call-update) | async-done | bytes 2359312 | tf_op jit(solution)/shard_map/all_gather | solution.py:77
  160.5 0.0 reduce-scatter.3.cloned.1.call-update
  160.5 0.0 all-gather.11.cloned.1.call-start
  160.6 48.8 %reduce-scatter.3.cloned.1.call-done = bf16[128,1536]{1,0:T(8,128)(2,1)} async-done(((bf16[1024,1536]{1,0:T(8,128)(2,1)}), bf16[128,1536]{1,0:T(8,128)(2,1)}) %reduce-scatter.3.cloned.1.call-update) | async-done | bytes 393232 | tf_op jit(solution)/shard_map/reduce_scatter | solution.py:98
  209.3 0.0 copy-done.1
  209.3 1.2 convert_reduce_fusion
  210.6 0.3 fusion.10
  210.8 0.0 copy-done.2
  210.8 1.0 fusion.12
  211.9 0.0 all-gather.11.cloned.1.call-update
  211.9 0.0 reduce-scatter.5.cloned.1.call-start
  211.9 44.4 %all-gather.11.cloned.1.call-done = bf16[1024,1536]{1,0:T(8,128)(2,1)} async-done(((bf16[128,1536]{1,0:T(8,128)(2,1)}), bf16[1024,1536]{1,0:T(8,128)(2,1)}) %all-gather.11.cloned.1.call-update) | async-done | bytes 3145744 | tf_op jit(solution)/shard_map/all_gather | solution.py:103
  256.4 11.1 %convolution_convert_fusion = bf16[1024,1536]{1,0:T(8,128)(2,1)} fusion(bf16[768,1536]{0,1:T(8,128)(2,1)} %all-gather.9.cloned.1.call-done, bf16[1024,1536]{1,0:T(8,128)(2,1)} %all-gather.11.cloned.1.call-done, bf16[1536,768]{1,0:T(8,128)(2,1)} %all-gather.7.cloned.1.call-done), kind=kOutput, calls=%fused_computation | convolution fusion | flops 4837343232 | bytes 11010048 | tf_op jit(solution)/shard_map/dot_general | solution.py:106
  267.4 0.0 reduce-scatter.5.cloned.1.call-update
  267.4 45.6 %reduce-scatter.5.cloned.1.call-done = bf16[128,1536]{1,0:T(8,128)(2,1)} async-done(((bf16[1024,1536]{1,0:T(8,128)(2,1)}), bf16[128,1536]{1,0:T(8,128)(2,1)}) %reduce-scatter.5.cloned.1.call-update) | async-done | bytes 393232 | tf_op jit(solution)/shard_map/reduce_scatter | solution.py:107
  313.0 1.9 fusion.17
  (25 shorter events, 0.2 us)
Async XLA Ops:
  6.5 92.2 %copy-start = (bf16[192,1536]{1,0:T(8,128)(2,1)S(1)}, bf16[192,1536]{1,0:T(8,128)(2,1)}, u32[]{:S(2)}) copy-start(bf16[192,1536]{1,0:T(8,128)(2,1)} %param.22) | copy-start | bytes 1769476
  6.5 52.6 %all-gather.5.cloned.1.call-start = ((), (), s32[]{:S(2)}) async-start(), calls=%async_computation.2 | async-start | bytes 3538944 | tf_op jit(solution)/shard_map/all_gather | solution.py:75
  11.1 98.3 %all-gather.7.cloned.1.call-start = ((), (), s32[]{:S(2)}) async-start(), calls=%async_computation.3 | async-start | bytes 2433024 | tf_op jit(solution)/shard_map/all_gather | solution.py:76
  11.8 148.7 %all-gather.9.cloned.1.call-start = ((), (), s32[]{:S(2)}) async-start(), calls=%async_computation.4 | async-start | bytes 2433024 | tf_op jit(solution)/shard_map/all_gather | solution.py:77
  12.5 196.8 %reduce-scatter.3.cloned.1.call-start = ((), (), s32[]{:S(2)}) async-start(), calls=%async_computation.5 | async-start | bytes 3538944 | tf_op jit(solution)/shard_map/reduce_scatter | solution.py:98
  15.6 46.9 %copy-start.4 = (bf16[1536,192]{0,1:T(8,128)(2,1)S(1)}, bf16[1536,192]{0,1:T(8,128)(2,1)}, u32[]{:S(2)}) copy-start(bf16[1536,192]{0,1:T(8,128)(2,1)} %param.17) | copy-start | bytes 1769476
  59.1 3.4 %copy-start.3 = (bf16[1024,1536]{1,0:T(8,128)(2,1)S(1)}, bf16[1024,1536]{1,0:T(8,128)(2,1)}, u32[]{:S(2)}) copy-start(bf16[1024,1536]{1,0:T(8,128)(2,1)} %all-gather.5.cloned.1.call-done) | copy-start | bytes 9437188
  62.6 36.1 %copy-start.5 = (f32[192]{0:T(256)S(1)}, f32[192]{0:T(256)}, u32[]{:S(2)}) copy-start(f32[192]{0:T(256)} %param.21) | copy-start | bytes 2308
  62.6 36.1 %copy-start.6 = (f32[192]{0:T(256)S(1)}, f32[192]{0:T(256)}, u32[]{:S(2)}) copy-start(f32[192]{0:T(256)} %param.20) | copy-start | bytes 2308
  63.9 8.5 %collective-permute-start = (bf16[15,192]{0,1:T(8,128)(2,1)S(1)}, bf16[15,192]{0,1:T(8,128)(2,1)S(1)}, u32[]{:S(2)}, u32[]{:S(2)}) collective-permute-start(bf16[15,192]{0,1:T(8,128)(2,1)S(1)} %get-tuple-element.31), channel_id=1, source_target_pairs={{0,8},{8,16},{16,24},{24,32},{32,40},{40,48},{48,56},{56,64},{64,7... | collective-permute-start | bytes 17288 | tf_op jit(solution)/shard_map/ppermute | solution.py:16
  65.8 6.6 %collective-permute-start.1 = (bf16[15,192]{0,1:T(8,128)(2,1)S(1)}, bf16[15,192]{0,1:T(8,128)(2,1)S(1)}, u32[]{:S(2)}, u32[]{:S(2)}) collective-permute-start(bf16[15,192]{0,1:T(8,128)(2,1)S(1)} %get-tuple-element.32), channel_id=1, source_target_pairs={{8,0},{16,8},{24,16},{32,24},{40,32},{48,40},{56,48},{64,56},{72,6... | collective-permute-start | bytes 17288 | tf_op jit(solution)/shard_map/ppermute | solution.py:17
  78.3 1.2 collective-permute-start.2
  79.7 3.7 %collective-permute-start.3 = (f32[3,192]{1,0:T(4,128)S(1)}, f32[3,192]{1,0:T(4,128)S(1)}, u32[]{:S(2)}, u32[]{:S(2)}) collective-permute-start(f32[3,192]{1,0:T(4,128)S(1)} %pad_maximum_fusion.3), channel_id=1, source_target_pairs={{0,16},{8,24},{16,0},{24,8},{32,48},{40,56},{48,32},{56,40},{64,80... | collective-permute-start | bytes 6920 | tf_op jit(solution)/shard_map/ppermute | solution.py:46
  83.5 5.9 %collective-permute-start.4 = (f32[3,192]{1,0:T(4,128)S(1)}, f32[3,192]{1,0:T(4,128)S(1)}, u32[]{:S(2)}, u32[]{:S(2)}) collective-permute-start(f32[3,192]{1,0:T(4,128)S(1)} %pad_maximum_fusion.4), channel_id=1, source_target_pairs={{0,32},{8,40},{16,48},{24,56},{32,0},{40,8},{48,16},{56,24},{64,96... | collective-permute-start | bytes 6920 | tf_op jit(solution)/shard_map/ppermute | solution.py:46
  89.4 3.7 %collective-permute-start.5 = (f32[3,192]{1,0:T(4,128)S(1)}, f32[3,192]{1,0:T(4,128)S(1)}, u32[]{:S(2)}, u32[]{:S(2)}) collective-permute-start(f32[3,192]{1,0:T(4,128)S(1)} %pad_maximum_fusion.5), channel_id=1, source_target_pairs={{0,64},{8,72},{16,80},{24,88},{32,96},{40,104},{48,112},{56,120},{... | collective-permute-start | bytes 6920 | tf_op jit(solution)/shard_map/ppermute | solution.py:46
  93.2 5.5 %collective-permute-start.6 = (f32[3,192]{1,0:T(4,128)S(1)}, f32[3,192]{1,0:T(4,128)S(1)}, u32[]{:S(2)}, u32[]{:S(2)}) collective-permute-start(f32[3,192]{1,0:T(4,128)S(1)} %pad_maximum_fusion.6), channel_id=1, source_target_pairs={{0,128},{8,136},{16,144},{24,152},{32,160},{40,168},{48,176},{56,1... | collective-permute-start | bytes 6920 | tf_op jit(solution)/shard_map/ppermute | solution.py:46
  101.6 107.8 %copy-start.1 = (bf16[128,1536]{1,0:T(8,128)(2,1)S(1)}, bf16[128,1536]{1,0:T(8,128)(2,1)}, u32[]{:S(2)}) copy-start(bf16[128,1536]{1,0:T(8,128)(2,1)} %param.13) | copy-start | bytes 1179652
  101.6 109.2 %copy-start.2 = (f32[1536]{0:T(1024)S(1)}, f32[1536]{0:T(1024)}, u32[]{:S(2)}) copy-start(f32[1536]{0:T(1024)} %param.23) | copy-start | bytes 18436
  160.5 95.9 %all-gather.11.cloned.1.call-start = ((), (), s32[]{:S(2)}) async-start(), calls=%async_computation.6 | async-start | bytes 3538944 | tf_op jit(solution)/shard_map/all_gather | solution.py:103
  211.9 101.1 %reduce-scatter.5.cloned.1.call-start = ((), (), s32[]{:S(2)}) async-start(), calls=%async_computation.7 | async-start | bytes 3538944 | tf_op jit(solution)/shard_map/reduce_scatter | solution.py:107
Sparse Core Ops, SparseCore 0:
  11.2 47.9 all-gather.4
  61.7 47.5 all-gather.6
  111.8 48.5 all-gather.8
  162.9 46.4 reduce-scatter.2
  212.0 44.3 all-gather.10
  267.6 45.4 reduce-scatter.4
where the time goes:
time: 322 us
  waiting for transfers between devices  253 us (79%)
  matrix products  18.5 us (6%)
  other arithmetic  16.4 us (5%)
  starting transfers between devices  15.9 us (5%)
  between operations  15.7 us (5%)
    all_gather x1, waiting for transfers between devices, shards(): down_whole = lax.all_gather(down_weight, 'tm', axis=1, tiled=True)  51.2 us
    reduce_scatter x1, waiting for transfers between devices, shards(): lax.psum_scatter(conv_part.astype(jnp.bfloat16), 'tensor', scatter_dimens...  48.8 us
    reduce_scatter x1, waiting for transfers between devices, shards(): lax.psum_scatter(partial_out.astype(jnp.bfloat16), 'tensor', scatter_dime...  45.6 us
    all_gather x1, waiting for transfers between devices, shards(): feed_block = lax.all_gather(feed_normed, 'tensor', axis=0, tiled=True)  44.4 us
    all_gather x1, waiting for transfers between devices, shards(): piece = lax.all_gather(normed, 'tensor', axis=0, tiled=True)  43.5 us
    dot_general x1, matrix products, shards(): jnp.dot(hidden, down_whole, preferred_element_type=jnp.float32)  11.1 us
    ppermute x5, starting transfers between devices, moments_over(): other = lax.ppermute(stats, axis, pairs)  10.1 us
    ppermute x5, waiting for transfers between devices, moments_over(): other = lax.ppermute(stats, axis, pairs)  9.85 us
  transfers between devices with their start and end apart: 13, of which 11 were waited for; matrix products, arithmetic and copies ran while one was open for 6% of the time, Pallas kernels for 0%

commit v1 on v0

--- a/solution.py
+++ b/solution.py
@@ -100,7 +100,9 @@
     ).astype(jnp.float32)
     mid = (features.astype(jnp.float32) + conv_out).astype(jnp.bfloat16)
     feed_normed = layer_norm(mid, feed_gain).astype(jnp.bfloat16)
-    feed_block = lax.all_gather(feed_normed, "tensor", axis=0, tiled=True)
+    feed_block = jnp.concatenate(
+        lax.all_to_all(jnp.stack([feed_normed] * lax.axis_size("tensor")), "tensor", 0, 0), axis=0
+    )
     pre = jnp.dot(feed_block, up_whole, preferred_element_type=jnp.float32)
     hidden = (pre * jax.nn.sigmoid(pre)).astype(jnp.bfloat16)
     partial_out = jnp.dot(hidden, down_whole, preferred_element_type=jnp.float32)

time: 322 us -> 350 us (1.087)
  blocking collectives: 0 us -> 76.4 us
  waiting for transfers between devices: 253 us -> 206 us
    all_to_all x0 -> x1, blocking collectives: none -> 76.4 us  [shards(): lax.all_to_all(jnp.stack([feed_normed] * lax.axis_size('tensor')), 'tenso...]
    all_gather x1 -> x0, waiting for transfers between devices: 44.4 us -> none  [shards(): feed_block = lax.all_gather(feed_normed, 'tensor', axis=0, tiled=True)]
  transfers between devices with their start and end apart: 13 -> 12, of which waited for: 11 -> 10; matrix products, arithmetic and copies ran while one was open for 6% -> 5% of each run, Pallas kernels for 0% -> 0%
where the time goes in v1:
time: 350 us; the launch traced here: 349 us
  waiting for transfers between devices  206 us (59%)
  blocking collectives  76.4 us (22%)
  matrix products  17.2 us (5%)
  starting transfers between devices  15.8 us (5%)
  other arithmetic  15.7 us (4%)
  between operations  15.3 us (4%)
    all_to_all x1, blocking collectives, shards(): lax.all_to_all(jnp.stack([feed_normed] * lax.axis_size('tensor')), 'tenso...  76.4 us
    all_gather x1, waiting for transfers between devices, shards(): down_whole = lax.all_gather(down_weight, 'tm', axis=1, tiled=True)  51.2 us
    reduce_scatter x1, waiting for transfers between devices, shards(): lax.psum_scatter(conv_part.astype(jnp.bfloat16), 'tensor', scatter_dimens...  48.8 us
    all_gather x1, waiting for transfers between devices, shards(): piece = lax.all_gather(normed, 'tensor', axis=0, tiled=True)  43.5 us
    reduce_scatter x1, waiting for transfers between devices, shards(): lax.psum_scatter(partial_out.astype(jnp.bfloat16), 'tensor', scatter_dime...  43 us
    ppermute x5, starting transfers between devices, moments_over(): other = lax.ppermute(stats, axis, pairs)  10.1 us
    ppermute x5, waiting for transfers between devices, moments_over(): other = lax.ppermute(stats, axis, pairs)  9.85 us
    dot_general x1, matrix products, shards(): jnp.dot(hidden, down_whole, preferred_element_type=jnp.float32)  9.81 us
  transfers between devices with their start and end apart: 12, of which 10 were waited for; matrix products, arithmetic and copies ran while one was open for 5% of the time, Pallas kernels for 0%

profile of v1, /device:TPU:2, one launch (start us, length us, event | category | flops | bytes accessed | tf_op | source)
XLA Modules:
  0.0 349.0 jit_solution(9176615563717747247)
XLA Ops:
  6.5 0.0 copy-start
  6.5 0.0 all-gather.4.cloned.1.call-start
  6.5 1.2 convert_reduce_fusion.1
  7.7 1.2 fusion.13
  9.0 2.0 fusion.15
  11.0 0.0 all-gather.4.cloned.1.call-update
  11.1 0.0 all-gather.6.cloned.1.call-start
  11.1 0.7 all-gather.6.cloned.1.call-update
  11.8 0.0 all-gather.8.cloned.1.call-start
  11.8 0.7 all-gather.8.cloned.1.call-update
  12.5 0.0 reduce-scatter.3.cloned.1.call-start
  13.2 1.0 fusion.66
  14.3 1.4 fusion.63
  15.6 0.0 copy-start.5
  15.6 43.5 %all-gather.4.cloned.1.call-done = bf16[1024,1536]{1,0:T(8,128)(2,1)} async-done(((bf16[128,1536]{1,0:T(8,128)(2,1)}), bf16[1024,1536]{1,0:T(8,128)(2,1)}) %all-gather.4.cloned.1.call-update) | async-done | bytes 3145744 | tf_op jit(solution)/shard_map/all_gather | solution.py:75
  59.1 3.4 fusion.4
  62.5 0.0 copy-done.5
  62.6 0.0 copy-done.3
  62.6 0.0 copy-start.6
  62.6 0.0 copy-start.7
  62.6 1.2 fusion.5
  63.8 0.1 fusion.65
  63.9 1.9 collective-permute-start
  65.8 3.6 %collective-permute-start.1 = (bf16[15,192]{0,1:T(8,128)(2,1)S(1)}, bf16[15,192]{0,1:T(8,128)(2,1)S(1)}, u32[]{:S(2)}, u32[]{:S(2)}) collective-permute-start(bf16[15,192]{0,1:T(8,128)(2,1)S(1)} %get-tuple-element.32), channel_id=1, source_target_pairs={{8,0},{16,8},{24,16},{32,24},{40,32},{48,40},{56,48},{64,56},{72,6... | collective-permute-start | bytes 17288 | tf_op jit(solution)/shard_map/ppermute | solution.py:17
  69.4 1.0 fusion.67
  71.7 0.6 pad.12.clone
  72.3 0.0 collective-permute-done
  72.3 0.0 collective-permute-done.1
  72.4 5.6 %multiply_reduce_fusion.1 = (f32[192]{0:T(256)S(1)}, f32[1024,192]{0,1:T(8,128)S(1)}) fusion(f32[1024]{0:T(1024)S(1)} %get-tuple-element.28, f32[192]{0:T(256)S(1)} %bitcast.81, bf16[15,192]{0,1:T(8,128)(2,1)S(1)} %collective-permute-done.1, bf16[1024,192]{0,1:T(8,128)(2,1)S(1)} %fusion.5, f32[192]{0:T(256)S(1)} %bitcast.82, f32[192]{0:T(256)S(1)} %bitcast.53, ...), kind=kLoop, calls=%fused_computation.58 | loop fusion | flops 36175680 | bytes 1219840 | tf_op jit(solution)/shard_map/reduce_sum | solution.py:86
  78.0 0.3 multiply_reduce_fusion
  78.2 0.1 pad_maximum_fusion.2
  78.3 0.4 collective-permute-start.2
  78.7 0.8 collective-permute-done.2
  79.6 0.1 broadcast_select_fusion.1
  79.7 0.6 collective-permute-start.3
  80.3 3.1 collective-permute-done.3
  83.5 4.3 %collective-permute-start.4 = (f32[3,192]{1,0:T(4,128)S(1)}, f32[3,192]{1,0:T(4,128)S(1)}, u32[]{:S(2)}, u32[]{:S(2)}) collective-permute-start(f32[3,192]{1,0:T(4,128)S(1)} %pad_maximum_fusion.4), channel_id=1, source_target_pairs={{0,32},{8,40},{16,48},{24,56},{32,0},{40,8},{48,16},{56,24},{64,96... | collective-permute-start | bytes 6920 | tf_op jit(solution)/shard_map/ppermute | solution.py:46
  87.7 1.6 collective-permute-done.4
  89.4 1.6 collective-permute-start.5
  91.0 2.1 collective-permute-done.5
  93.2 3.2 collective-permute-start.6
  96.4 2.3 collective-permute-done.6
  98.7 0.0 copy-done
  98.7 0.0 copy-done.6
  98.7 0.0 copy-done.7
  98.7 2.9 fusion.18
  101.6 7.7 %all-gather.6.cloned.1.call-done = bf16[1536,768]{1,0:T(8,128)(2,1)} async-done(((bf16[48,768]{1,0:T(8,128)(2,1)}), bf16[1536,768]{1,0:T(8,128)(2,1)}) %all-gather.6.cloned.1.call-update) | async-done | bytes 2359312 | tf_op jit(solution)/shard_map/all_gather | solution.py:76
  109.3 51.2 %all-gather.8.cloned.1.call-done = bf16[768,1536]{0,1:T(8,128)(2,1)} async-done(((bf16[768,48]{0,1:T(8,128)(2,1)}), bf16[768,1536]{0,1:T(8,128)(2,1)}) %all-gather.8.cloned.1.call-update) | async-done | bytes 2359312 | tf_op jit(solution)/shard_map/all_gather | solution.py:77
  160.5 0.0 reduce-scatter.3.cloned.1.call-update
  160.5 0.0 reduce-scatter.5.cloned.1.call-start
  160.6 48.8 %reduce-scatter.3.cloned.1.call-done = bf16[128,1536]{1,0:T(8,128)(2,1)} async-done(((bf16[1024,1536]{1,0:T(8,128)(2,1)}), bf16[128,1536]{1,0:T(8,128)(2,1)}) %reduce-scatter.3.cloned.1.call-update) | async-done | bytes 393232 | tf_op jit(solution)/shard_map/reduce_scatter | solution.py:98
  209.3 0.0 copy-done.1
  209.3 1.2 convert_reduce_fusion
  210.6 0.3 fusion.10
  210.8 0.0 copy-done.2
  210.8 0.3 fusion.12
  211.1 0.3 stack.20
  211.4 0.0 copy-start.4
  211.4 76.4 %all_to_all.5 = bf16[8,128,1536]{2,1,0:T(8,128)(2,1)} all-to-all(bf16[8,128,1536]{2,1,0:T(8,128)(2,1)S(1)} %stack.20), channel_id=1, replica_groups=mesh['tm'=32,'tensor'=8] {'tensor'}, dimensions={0} | all-to-all | bytes 6291456 | tf_op jit(solution)/shard_map/all_to_all | solution.py:104
  287.8 0.0 copy-done.4
  287.8 9.8 %convolution_convert_fusion = bf16[1024,1536]{1,0:T(8,128)(2,1)} fusion(bf16[768,1536]{0,1:T(8,128)(2,1)} %all-gather.8.cloned.1.call-done, bf16[1024,1536]{1,0:T(8,128)(2,1)} %bitcast.47, bf16[1536,768]{1,0:T(8,128)(2,1)S(1)} %copy-done.4), kind=kOutput, calls=%fused_computation | convolution fusion | flops 4837343232 | bytes 11010048 | tf_op jit(solution)/shard_map/dot_general | solution.py:108
  297.6 0.0 reduce-scatter.5.cloned.1.call-update
  297.6 43.0 %reduce-scatter.5.cloned.1.call-done = bf16[128,1536]{1,0:T(8,128)(2,1)} async-done(((bf16[1024,1536]{1,0:T(8,128)(2,1)}), bf16[128,1536]{1,0:T(8,128)(2,1)}) %reduce-scatter.5.cloned.1.call-update) | async-done | bytes 393232 | tf_op jit(solution)/shard_map/reduce_scatter | solution.py:109
  340.7 1.9 fusion.17
  (26 shorter events, 0.2 us)
Async XLA Ops:
  6.5 92.2 %copy-start = (bf16[192,1536]{1,0:T(8,128)(2,1)S(1)}, bf16[192,1536]{1,0:T(8,128)(2,1)}, u32[]{:S(2)}) copy-start(bf16[192,1536]{1,0:T(8,128)(2,1)} %param.22) | copy-start | bytes 1769476
  6.5 52.6 %all-gather.4.cloned.1.call-start = ((), (), s32[]{:S(2)}) async-start(), calls=%async_computation.3 | async-start | bytes 3538944 | tf_op jit(solution)/shard_map/all_gather | solution.py:75
  11.1 98.3 %all-gather.6.cloned.1.call-start = ((), (), s32[]{:S(2)}) async-start(), calls=%async_computation.4 | async-start | bytes 2433024 | tf_op jit(solution)/shard_map/all_gather | solution.py:76
  11.8 148.7 %all-gather.8.cloned.1.call-start = ((), (), s32[]{:S(2)}) async-start(), calls=%async_computation.5 | async-start | bytes 2433024 | tf_op jit(solution)/shard_map/all_gather | solution.py:77
  12.5 196.8 %reduce-scatter.3.cloned.1.call-start = ((), (), s32[]{:S(2)}) async-start(), calls=%async_computation.6 | async-start | bytes 3538944 | tf_op jit(solution)/shard_map/reduce_scatter | solution.py:98
  15.6 46.9 %copy-start.5 = (bf16[1536,192]{0,1:T(8,128)(2,1)S(1)}, bf16[1536,192]{0,1:T(8,128)(2,1)}, u32[]{:S(2)}) copy-start(bf16[1536,192]{0,1:T(8,128)(2,1)} %param.17) | copy-start | bytes 1769476
  59.1 3.4 copy-start.3
  62.6 36.1 %copy-start.6 = (f32[192]{0:T(256)S(1)}, f32[192]{0:T(256)}, u32[]{:S(2)}) copy-start(f32[192]{0:T(256)} %param.21) | copy-start | bytes 2308
  62.6 36.1 %copy-start.7 = (f32[192]{0:T(256)S(1)}, f32[192]{0:T(256)}, u32[]{:S(2)}) copy-start(f32[192]{0:T(256)} %param.20) | copy-start | bytes 2308
  63.9 8.5 %collective-permute-start = (bf16[15,192]{0,1:T(8,128)(2,1)S(1)}, bf16[15,192]{0,1:T(8,128)(2,1)S(1)}, u32[]{:S(2)}, u32[]{:S(2)}) collective-permute-start(bf16[15,192]{0,1:T(8,128)(2,1)S(1)} %get-tuple-element.31), channel_id=1, source_target_pairs={{0,8},{8,16},{16,24},{24,32},{32,40},{40,48},{48,56},{56,64},{64,7... | collective-permute-start | bytes 17288 | tf_op jit(solution)/shard_map/ppermute | solution.py:16
  65.8 6.6 %collective-permute-start.1 = (bf16[15,192]{0,1:T(8,128)(2,1)S(1)}, bf16[15,192]{0,1:T(8,128)(2,1)S(1)}, u32[]{:S(2)}, u32[]{:S(2)}) collective-permute-start(bf16[15,192]{0,1:T(8,128)(2,1)S(1)} %get-tuple-element.32), channel_id=1, source_target_pairs={{8,0},{16,8},{24,16},{32,24},{40,32},{48,40},{56,48},{64,56},{72,6... | collective-permute-start | bytes 17288 | tf_op jit(solution)/shard_map/ppermute | solution.py:17
  78.3 1.2 collective-permute-start.2
  79.7 3.7 %collective-permute-start.3 = (f32[3,192]{1,0:T(4,128)S(1)}, f32[3,192]{1,0:T(4,128)S(1)}, u32[]{:S(2)}, u32[]{:S(2)}) collective-permute-start(f32[3,192]{1,0:T(4,128)S(1)} %pad_maximum_fusion.3), channel_id=1, source_target_pairs={{0,16},{8,24},{16,0},{24,8},{32,48},{40,56},{48,32},{56,40},{64,80... | collective-permute-start | bytes 6920 | tf_op jit(solution)/shard_map/ppermute | solution.py:46
  83.5 5.9 %collective-permute-start.4 = (f32[3,192]{1,0:T(4,128)S(1)}, f32[3,192]{1,0:T(4,128)S(1)}, u32[]{:S(2)}, u32[]{:S(2)}) collective-permute-start(f32[3,192]{1,0:T(4,128)S(1)} %pad_maximum_fusion.4), channel_id=1, source_target_pairs={{0,32},{8,40},{16,48},{24,56},{32,0},{40,8},{48,16},{56,24},{64,96... | collective-permute-start | bytes 6920 | tf_op jit(solution)/shard_map/ppermute | solution.py:46
  89.4 3.7 %collective-permute-start.5 = (f32[3,192]{1,0:T(4,128)S(1)}, f32[3,192]{1,0:T(4,128)S(1)}, u32[]{:S(2)}, u32[]{:S(2)}) collective-permute-start(f32[3,192]{1,0:T(4,128)S(1)} %pad_maximum_fusion.5), channel_id=1, source_target_pairs={{0,64},{8,72},{16,80},{24,88},{32,96},{40,104},{48,112},{56,120},{... | collective-permute-start | bytes 6920 | tf_op jit(solution)/shard_map/ppermute | solution.py:46
  93.2 5.5 %collective-permute-start.6 = (f32[3,192]{1,0:T(4,128)S(1)}, f32[3,192]{1,0:T(4,128)S(1)}, u32[]{:S(2)}, u32[]{:S(2)}) collective-permute-start(f32[3,192]{1,0:T(4,128)S(1)} %pad_maximum_fusion.6), channel_id=1, source_target_pairs={{0,128},{8,136},{16,144},{24,152},{32,160},{40,168},{48,176},{56,1... | collective-permute-start | bytes 6920 | tf_op jit(solution)/shard_map/ppermute | solution.py:46
  101.6 107.8 %copy-start.1 = (bf16[128,1536]{1,0:T(8,128)(2,1)S(1)}, bf16[128,1536]{1,0:T(8,128)(2,1)}, u32[]{:S(2)}) copy-start(bf16[128,1536]{1,0:T(8,128)(2,1)} %param.13) | copy-start | bytes 1179652
  101.6 109.2 %copy-start.2 = (f32[1536]{0:T(1024)S(1)}, f32[1536]{0:T(1024)}, u32[]{:S(2)}) copy-start(f32[1536]{0:T(1024)} %param.23) | copy-start | bytes 18436
  160.5 180.1 %reduce-scatter.5.cloned.1.call-start = ((), (), s32[]{:S(2)}) async-start(), calls=%async_computation.7 | async-start | bytes 3538944 | tf_op jit(solution)/shard_map/reduce_scatter | solution.py:109
  211.4 76.4 %copy-start.4 = (bf16[1536,768]{1,0:T(8,128)(2,1)S(1)}, bf16[1536,768]{1,0:T(8,128)(2,1)}, u32[]{:S(2)}) copy-start(bf16[1536,768]{1,0:T(8,128)(2,1)} %all-gather.6.cloned.1.call-done) | copy-start | bytes 7077892
Sparse Core Ops, SparseCore 0:
  11.2 47.9 all-gather.3
  61.7 47.5 all-gather.5
  111.8 48.5 all-gather.7
  162.9 46.4 reduce-scatter.2
  297.7 42.8 reduce-scatter.4
